TPU v7x, 512 devices: a whole 4x8x8 slice. The times are simulated.
512 devices in a mesh: dp: 32 (over z, y_lo, core), feat: 16 (over y_hi, x).
Axes of the slice: x: 4, y: 8 (y_hi: 4, y_lo: 2; y = y_hi * 2 + y_lo), z: 8, core: 2. Of those that a mesh axis runs over, the one named last changes fastest.
Arguments:
- tokens: bfloat16 [8192, 8192], P('dp', 'feat'), may hold values from -6 to 6
- up_left: bfloat16 [16, 512, 2048], P('feat', 'dp'), may hold values from -0.25 to 0.25
- up_right: bfloat16 [2048, 16, 16], P('feat'), may hold values from -1.5 to 1.5
- down_left: bfloat16 [16, 2048, 512], P('feat', 'dp'), may hold values from -0.125 to 0.125
- down_right: bfloat16 [512, 16, 16], P('feat'), may hold values from -1.5 to 1.5
- layer_grad: bfloat16 [8192, 8192], P('dp', 'feat'), may hold values from -6 to 6
Outputs:
- layer_out: bfloat16 [8192, 8192], P('dp', 'feat')
- grad_tokens: bfloat16 [8192, 8192], P('dp', 'feat')
- grad_up_left: float32 [16, 512, 2048], P('feat', 'dp')
- grad_up_right: float32 [2048, 16, 16], P('feat')
- grad_down_left: float32 [16, 2048, 512], P('feat', 'dp')
- grad_down_right: float32 [512, 16, 16], P('feat')
All inputs are finite; a program needn't handle non-finite values.
Results may differ from a plain program's by a relative error of at most 0.0067.
Values may be sent and summed in bfloat16 or wider, within the bound.
No kernel may reach another device: no remote copies, remote signals or barrier semaphores. Data moves between devices by JAX's collectives and lax.ppermute only.
A program may use at most 128 MiB of HBM per device.

v0:
```python
import jax
import jax.numpy as jnp
import numpy as np
from jax import lax
from jax.sharding import Mesh
from jax.sharding import PartitionSpec as P

TILE_UP = 128
TILE_DOWN = 32
DP_AXES = ("z", "ylo", "core")
FEAT_AXES = ("yhi", "x")


def split_mesh(mesh):
    n_dp = mesh.shape["dp"]
    n_feat = mesh.shape["feat"]
    sizes = (n_dp // 4, 2, 2, n_feat // 4, 4)
    devices = np.asarray(mesh.devices).reshape(sizes)
    return Mesh(devices, DP_AXES + FEAT_AXES)


def exchange(wired):
    rows, feat_count, piece = wired.shape
    n_x = lax.axis_size("x")
    n_y = feat_count // n_x
    shaped = wired.reshape(rows, n_y, n_x, piece)
    shaped = lax.all_to_all(shaped, "x", 2, 2, tiled=True)
    shaped = lax.all_to_all(shaped, "yhi", 1, 1, tiled=True)
    return shaped.reshape(rows, feat_count, piece)


def dp_reduce_scatter(part, row_axis):
    shape = part.shape
    rows = shape[row_axis]
    n_z = lax.axis_size("z")
    split = shape[:row_axis] + (n_z, 2, 2, rows // (4 * n_z)) + shape[row_axis + 1 :]
    x = part.reshape(split)
    x = lax.psum_scatter(x, "core", scatter_dimension=row_axis + 2, tiled=True)
    x = lax.psum_scatter(x, "z", scatter_dimension=row_axis, tiled=True)
    x = lax.psum_scatter(x, "ylo", scatter_dimension=row_axis + 1, tiled=True)
    return x.reshape(shape[:row_axis] + (rows // (4 * n_z),) + shape[row_axis + 1 :])


def dp_all_gather(local, row_axis):
    shape = local.shape
    rows = shape[row_axis]
    x = local.reshape(shape[:row_axis] + (1, 1, 1, rows) + shape[row_axis + 1 :])
    x = lax.all_gather(x, "ylo", axis=row_axis + 1, tiled=True)
    x = lax.all_gather(x, "z", axis=row_axis, tiled=True)
    x = lax.all_gather(x, "core", axis=row_axis + 2, tiled=True)
    total = x.shape[row_axis] * x.shape[row_axis + 1] * x.shape[row_axis + 2] * rows
    return x.reshape(shape[:row_axis] + (total,) + shape[row_axis + 1 :])


def to_wire(blocks, feat_count):
    tok_rows, local_blocks, full_width = blocks.shape
    piece = full_width // feat_count
    shaped = blocks.reshape(tok_rows, local_blocks, feat_count, piece).transpose(0, 2, 1, 3)
    return shaped.reshape(tok_rows, feat_count, local_blocks * piece)


def from_wire(wired, local_blocks):
    tok_rows, feat_count, line_len = wired.shape
    piece = line_len // local_blocks
    shaped = wired.reshape(tok_rows, feat_count, local_blocks, piece).transpose(0, 2, 1, 3)
    return shaped.reshape(tok_rows, local_blocks, feat_count * piece)


def on_device(tokens, up_left, up_right, down_left, down_right, layer_grad):
    tok_rows = tokens.shape[0]
    local_blocks = up_left.shape[0]
    hidden_width = up_left.shape[2]
    block_width = down_left.shape[2]
    blocks_all = up_right.shape[1]
    group_up = up_right.shape[0]
    group_down = down_right.shape[0]
    feat_count = lax.axis_size("yhi") * lax.axis_size("x")
    n_dp = lax.axis_size("z") * lax.axis_size("ylo") * lax.axis_size("core")
    grad_scale = float(tok_rows * n_dp) ** (-0.5)
    tiles_up = group_up // TILE_UP
    tiles_down = group_down // TILE_DOWN
    up_full = dp_all_gather(up_left, 1)
    token_blocks = tokens.reshape(tok_rows, local_blocks, block_width)
    up_inner = jnp.einsum(
        "tbi,big->tbg", token_blocks, up_full, preferred_element_type=jnp.float32
    ).astype(jnp.bfloat16)
    up_mixed = exchange(to_wire(up_inner, feat_count))
    preact = jnp.einsum("tjg,gjk->tkg", up_mixed, up_right, preferred_element_type=jnp.float32)
    sigmoid_val = jax.nn.sigmoid(preact)
    activated = (
        (preact * sigmoid_val)
        .reshape(tok_rows, blocks_all, tiles_up, TILE_UP)
        .transpose(0, 2, 1, 3)
    )
    hidden = activated.reshape(tok_rows, local_blocks, hidden_width).astype(jnp.bfloat16)
    down_full = dp_all_gather(down_left, 1)
    down_inner = jnp.einsum(
        "tbh,bhc->tbc", hidden, down_full, preferred_element_type=jnp.float32
    ).astype(jnp.bfloat16)
    down_mixed = exchange(to_wire(down_inner, feat_count)).reshape(
        tok_rows, blocks_all * group_down
    )
    identity = jnp.eye(group_down, dtype=jnp.bfloat16).reshape(group_down, tiles_down, TILE_DOWN)
    mix_matrix = jnp.einsum(
        "cjk,cal->jcakl", down_right, identity, preferred_element_type=jnp.float32
    )
    mix_matrix = mix_matrix.astype(jnp.bfloat16).reshape(
        blocks_all * group_down, blocks_all * group_down
    )
    layer_out = jnp.dot(down_mixed, mix_matrix, preferred_element_type=jnp.float32).astype(
        jnp.bfloat16
    )
    grad_down_mixed = lax.dot_general(
        layer_grad, mix_matrix, (((1,), (1,)), ((), ())), preferred_element_type=jnp.float32
    ).astype(jnp.bfloat16)
    grad_by_group = layer_grad.reshape(tok_rows, tiles_down, blocks_all, TILE_DOWN).transpose(
        0, 2, 1, 3
    )
    grad_by_group = grad_by_group.reshape(tok_rows, blocks_all, group_down)
    right_down_term = (
        jnp.einsum(
            "tjc,tkc->cjk",
            down_mixed.reshape(tok_rows, blocks_all, group_down),
            grad_by_group,
            preferred_element_type=jnp.float32,
        )
        * grad_scale
    )
    grad_down_inner = from_wire(
        exchange(grad_down_mixed.reshape(tok_rows, feat_count, local_blocks * group_down)),
        local_blocks,
    )
    grad_down_left = dp_reduce_scatter(
        jnp.einsum("tbh,tbc->hbc", hidden, grad_down_inner, preferred_element_type=jnp.float32)
        * grad_scale,
        0,
    ).transpose(1, 0, 2)
    grad_hidden = jnp.einsum(
        "tbc,bhc->tbh", grad_down_inner, down_full, preferred_element_type=jnp.float32
    )
    grad_hidden = grad_hidden.reshape(tok_rows, tiles_up, blocks_all, TILE_UP).transpose(0, 2, 1, 3)
    grad_hidden = grad_hidden.reshape(tok_rows, blocks_all, group_up)
    grad_preact = (grad_hidden * sigmoid_val * (1.0 + preact * (1.0 - sigmoid_val))).astype(
        jnp.bfloat16
    )
    grad_up_mixed = jnp.einsum(
        "tkg,gjk->tjg", grad_preact, up_right, preferred_element_type=jnp.float32
    ).astype(jnp.bfloat16)
    right_up_term = (
        jnp.einsum("tjg,tkg->gjk", up_mixed, grad_preact, preferred_element_type=jnp.float32)
        * grad_scale
    )
    grad_up_inner = from_wire(exchange(grad_up_mixed), local_blocks)
    grad_tokens = jnp.einsum(
        "tbg,big->tbi", grad_up_inner, up_full, preferred_element_type=jnp.float32
    ).astype(jnp.bfloat16)
    grad_tokens = grad_tokens.reshape(tok_rows, local_blocks * block_width)
    grad_up_left = dp_reduce_scatter(
        jnp.einsum("tbi,tbg->ibg", token_blocks, grad_up_inner, preferred_element_type=jnp.float32)
        * grad_scale,
        0,
    ).transpose(1, 0, 2)
    rights = jnp.concatenate([right_up_term, right_down_term], axis=0)
    rights = lax.psum(rights, DP_AXES)
    grad_up_right = rights[:group_up]
    grad_down_right = rights[group_up:]
    return (layer_out, grad_tokens, grad_up_left, grad_up_right, grad_down_left, grad_down_right)


def solution(mesh):
    fine = split_mesh(mesh)
    row = P(DP_AXES, FEAT_AXES)
    weight = P(FEAT_AXES, DP_AXES, None)
    mixer = P(FEAT_AXES, None, None)
    return jax.shard_map(
        on_device,
        mesh=fine,
        in_specs=(row, weight, mixer, weight, mixer, row),
        out_specs=(row, row, weight, mixer, weight, mixer),
        check_vma=False,
    )
```

profile of v0, /device:TPU:1, one launch (start us, length us, event | category | flops | bytes accessed | tf_op | source)
XLA Modules:
  0.0 650.3 jit_solution(2913419054008153790)
XLA Ops:
  7.2 6.3 all-gather
  13.6 42.4 %all-gather.13.cloned.1.call-done = bf16[16,16,2048]{2,1,0:T(8,128)(2,1)} async-done(((bf16[2,16,2048]{2,1,0:T(8,128)(2,1)}), bf16[16,16,2048]{2,1,0:T(8,128)(2,1)}) %all-gather.13.cloned.1.call-update) | async-done | bytes 1048592 | tf_op jit(solution)/shard_map/all_gather | solution.py:49
  56.1 5.3 all-gather.2
  66.9 4.0 all-to-all-start.4
  70.8 10.1 %all-gather.9.cloned.1.call-done = bf16[1,8,2,2,16,2048]{5,4,3,2,1,0:T(8,128)(2,1)} async-done(((bf16[1,8,2,1,16,2048]{5,4,3,2,1,0:T(8,128)(2,1)}), bf16[1,8,2,2,16,2048]{5,4,3,2,1,0:T(8,128)(2,1)}) %all-gather.9.cloned.1.call-update) | async-done | bytes 2097168 | tf_op jit(solution)/shard_map/all_gather | solution.py:50
  80.9 2.3 convolution_convert_fusion
  84.4 3.5 all-to-all-start
  87.9 32.6 %all-gather.15.cloned.1.call-done = bf16[16,64,512]{2,1,0:T(8,128)(2,1)} async-done(((bf16[2,64,512]{2,1,0:T(8,128)(2,1)}), bf16[16,64,512]{2,1,0:T(8,128)(2,1)}) %all-gather.15.cloned.1.call-update) | async-done | bytes 1048592 | tf_op jit(solution)/shard_map/all_gather | solution.py:49
  121.3 6.5 all-to-all-start.5
  128.8 6.9 %all-to-all-done.5 = bf16[256,4,4,32]{0,3,2,1:T(8,128)(2,1)S(1)} async-done(((bf16[256,4,4,32]{0,3,2,1:T(8,128)(2,1)}), bf16[256,4,4,32]{0,3,2,1:T(8,128)(2,1)S(1)}, u32[]{:S(2)}, u32[]{:S(2)}) %all-to-all-start.5) | async-done | bytes 262176 | tf_op jit(solution)/shard_map/all_to_all | solution.py:28
  135.7 4.3 all-to-all-start.1
  141.2 4.1 all-gather.11.cloned.1.call-done
  147.6 18.1 %all-to-all-done.1 = bf16[256,4,4,128]{0,3,2,1:T(8,128)(2,1)} async-done(((bf16[256,4,4,128]{0,3,2,1:T(8,128)(2,1)}), bf16[256,4,4,128]{0,3,2,1:T(8,128)(2,1)}, u32[]{:S(2)}, u32[]{:S(2)}) %all-to-all-start.1) | async-done | bytes 1048608 | tf_op jit(solution)/shard_map/all_to_all | solution.py:28
  165.8 4.5 fusion.7
  172.3 15.0 %all_to_all.40 = bf16[256,4,4,128]{0,3,1,2:T(8,128)(2,1)S(1)} all-to-all(bf16[256,4,4,128]{0,3,1,2:T(8,128)(2,1)S(1)} %copy.95), channel_id=1, replica_groups=mesh['z'=8,'ylo'=2,'core'=2,'yhi'=4,'x'=4] {'x'}, dimensions={2} | all-to-all | bytes 2097152 | tf_op jit(solution)/shard_map/all_to_all | solution.py:27
  188.4 6.5 %all-to-all-start.7 = ((bf16[256,4,4,128]{0,3,2,1:T(8,128)(2,1)}), bf16[256,4,4,128]{0,3,2,1:T(8,128)(2,1)S(1)}, u32[]{:S(2)}, u32[]{:S(2)}) async-start(bf16[256,4,4,128]{0,3,2,1:T(8,128)(2,1)} %copy.96), calls=%async_computation.7 | async-start | bytes 2097152 | tf_op jit(solution)/shard_map/all_to_all | solution.py:28
  196.3 2.7 multiply_bitcast_fusion
  199.0 5.4 copy.103
  204.5 10.2 %all-to-all-done.7 = bf16[256,4,4,128]{0,3,2,1:T(8,128)(2,1)S(1)} async-done(((bf16[256,4,4,128]{0,3,2,1:T(8,128)(2,1)}), bf16[256,4,4,128]{0,3,2,1:T(8,128)(2,1)S(1)}, u32[]{:S(2)}, u32[]{:S(2)}) %all-to-all-start.7) | async-done | bytes 1048608 | tf_op jit(solution)/shard_map/all_to_all | solution.py:28
  214.7 2.7 convolution_multiply_fusion
  218.7 53.0 %all-reduce.8.cloned.1.call-done = (f32[8,2,2,16,1,2048]{5,3,4,2,1,0:T(8,128)}, f32[8,2,2,64,1,512]{5,3,2,1,0,4:T(8,128)}) async-done(((f32[8,2,2,16,1,2048]{5,3,4,2,1,0:T(8,128)}, f32[8,2,2,64,1,512]{5,3,2,1,0,4:T(8,128)}), (f32[8,2,2,16,1,2048]{5,3,4,2,1,0:T(8,128)}, f32[8,2,2,64,1,512]{5,3,2,1,0,4:T(8,128)})) %all-reduce.8.cloned.1.call-update) | async-done | bytes 8388624
  271.7 3.9 constant_dynamic-slice_fusion
  275.6 3.9 constant_dynamic-slice_fusion.1
  283.2 9.2 %all_to_all.41 = bf16[256,4,4,32]{0,3,1,2:T(8,128)(2,1)S(1)} all-to-all(bf16[256,4,4,32]{0,3,1,2:T(8,128)(2,1)S(1)} %copy.87), channel_id=1, replica_groups=mesh['z'=8,'ylo'=2,'core'=2,'yhi'=4,'x'=4] {'x'}, dimensions={2} | all-to-all | bytes 524288 | tf_op jit(solution)/shard_map/all_to_all | solution.py:27
  293.1 6.5 all-to-all-start.3
  302.9 5.1 all-to-all-done.3
  309.3 7.6 %reduce-scatter.13.cloned.1.call-done = f32[1,2,1,64,1,512]{5,3,2,1,0,4:T(8,128)} async-done(((f32[8,2,1,64,1,512]{5,3,2,1,0,4:T(8,128)}), f32[1,2,1,64,1,512]{5,3,2,1,0,4:T(8,128)}) %reduce-scatter.13.cloned.1.call-update) | async-done | bytes 262160 | tf_op jit(solution)/shard_map/reduce_scatter | solution.py:39
  317.0 46.2 %reduce-scatter.9.cloned.1.call-done = f32[1,2,1,16,1,2048]{5,3,4,2,1,0:T(8,128)} async-done(((f32[8,2,1,16,1,2048]{5,3,4,2,1,0:T(8,128)}), f32[1,2,1,16,1,2048]{5,3,4,2,1,0:T(8,128)}) %reduce-scatter.9.cloned.1.call-update) | async-done | bytes 262160 | tf_op jit(solution)/shard_map/reduce_scatter | solution.py:39
  364.3 233.1 %all-reduce.6.cloned.1.call-done = f32[160,16,16]{0,2,1:T(8,128)} async-done(((f32[160,16,16]{0,2,1:T(8,128)}), f32[160,16,16]{0,2,1:T(8,128)}) %all-reduce.6.cloned.1.call-update) | async-done | bytes 163856 | tf_op jit(solution)/shard_map/psum | solution.py:164
  600.6 3.0 convolution_convert_fusion.2
  603.6 16.7 %reduce-scatter.15.cloned.1.call-done = f32[1,1,1,64,1,512]{5,3,2,1,0,4:T(8,128)} async-done(((f32[1,2,1,64,1,512]{5,3,2,1,0,4:T(8,128)}), f32[1,1,1,64,1,512]{5,3,2,1,0,4:T(8,128)}) %reduce-scatter.15.cloned.1.call-update) | async-done | bytes 131088 | tf_op jit(solution)/shard_map/reduce_scatter | solution.py:40
  620.3 23.2 %reduce-scatter.11.cloned.1.call-done = f32[1,1,1,16,1,2048]{5,3,4,2,1,0:T(8,128)} async-done(((f32[1,2,1,16,1,2048]{5,3,4,2,1,0:T(8,128)}), f32[1,1,1,16,1,2048]{5,3,4,2,1,0:T(8,128)}) %reduce-scatter.11.cloned.1.call-update) | async-done | bytes 131088 | tf_op jit(solution)/shard_map/reduce_scatter | solution.py:40
  (76 shorter events, 31.2 us)
Async XLA Ops:
  7.2 73.8 %copy-start = (bf16[256,512]{1,0:T(8,128)(2,1)S(1)}, bf16[256,512]{1,0:T(8,128)(2,1)}, u32[]{:S(2)}) copy-start(bf16[256,512]{1,0:T(8,128)(2,1)} %param.6) | copy-start | bytes 786436
  7.2 48.8 %all-gather.13.cloned.1.call-start = ((), (), s32[]{:S(2)}) async-start(), calls=%async_computation.19 | async-start | bytes 1179648 | tf_op jit(solution)/shard_map/all_gather | solution.py:49
  13.6 67.3 %all-gather.9.cloned.1.call-start = ((), (), s32[]{:S(2)}) async-start(), calls=%async_computation.12 | async-start | bytes 3145728 | tf_op jit(solution)/shard_map/all_gather | solution.py:50
  56.0 64.5 %all-gather.15.cloned.1.call-start = ((), (), s32[]{:S(2)}) async-start(), calls=%async_computation.20 | async-start | bytes 1179648 | tf_op jit(solution)/shard_map/all_gather | solution.py:49
  62.3 3.5 copy-start.9
  66.9 17.5 %all-to-all-start.4 = ((bf16[256,4,4,32]{0,3,1,2:T(8,128)(2,1)}), bf16[256,4,4,32]{0,3,1,2:T(8,128)(2,1)S(1)}, u32[]{:S(2)}, u32[]{:S(2)}) async-start(bf16[256,4,4,32]{0,3,1,2:T(8,128)(2,1)} %copy.90), calls=%async_computation.4 | async-start | bytes 524288 | tf_op jit(solution)/shard_map/all_to_all | solution.py:27
  84.4 37.0 %all-to-all-start = ((bf16[256,4,4,128]{0,3,1,2:T(8,128)(2,1)}), bf16[256,4,4,128]{0,3,1,2:T(8,128)(2,1)S(1)}, u32[]{:S(2)}, u32[]{:S(2)}) async-start(bf16[256,4,4,128]{0,3,1,2:T(8,128)(2,1)} %copy.81), calls=%async_computation | async-start | bytes 2097152 | tf_op jit(solution)/shard_map/all_to_all | solution.py:27
  87.9 57.4 %all-gather.11.cloned.1.call-start = ((), (), s32[]{:S(2)}) async-start(), calls=%async_computation.13 | async-start | bytes 3145728 | tf_op jit(solution)/shard_map/all_gather | solution.py:50
  121.3 14.4 %all-to-all-start.5 = ((bf16[256,4,4,32]{0,3,2,1:T(8,128)(2,1)}), bf16[256,4,4,32]{0,3,2,1:T(8,128)(2,1)S(1)}, u32[]{:S(2)}, u32[]{:S(2)}) async-start(bf16[256,4,4,32]{0,3,2,1:T(8,128)(2,1)} %copy.91), calls=%async_computation.5 | async-start | bytes 524288 | tf_op jit(solution)/shard_map/all_to_all | solution.py:28
  127.8 12.2 %copy-start.11 = (bf16[128,16,16]{0,2,1:T(8,128)(2,1)S(1)}, bf16[128,16,16]{0,2,1:T(8,128)(2,1)}, u32[]{:S(2)}) copy-start(bf16[128,16,16]{0,2,1:T(8,128)(2,1)} %param.8) | copy-start | bytes 196612
  135.7 30.0 %all-to-all-start.1 = ((bf16[256,4,4,128]{0,3,2,1:T(8,128)(2,1)}), bf16[256,4,4,128]{0,3,2,1:T(8,128)(2,1)}, u32[]{:S(2)}, u32[]{:S(2)}) async-start(bf16[256,4,4,128]{0,3,2,1:T(8,128)(2,1)} %copy.82), calls=%async_computation.1 | async-start | bytes 2097152 | tf_op jit(solution)/shard_map/all_to_all | solution.py:28
  165.7 5.5 copy-start.7
  170.2 1.0 copy-start.2
  187.3 7.6 %copy-start.8 = (bf16[256,16,128]{0,1,2:T(8,128)(2,1)S(1)}, bf16[256,16,128]{0,1,2:T(8,128)(2,1)}, u32[]{:S(2)}) copy-start(bf16[256,16,128]{0,1,2:T(8,128)(2,1)} %get-tuple-element.21) | copy-start | bytes 3145732
  188.4 26.3 %all-to-all-start.7 = ((bf16[256,4,4,128]{0,3,2,1:T(8,128)(2,1)}), bf16[256,4,4,128]{0,3,2,1:T(8,128)(2,1)S(1)}, u32[]{:S(2)}, u32[]{:S(2)}) async-start(bf16[256,4,4,128]{0,3,2,1:T(8,128)(2,1)} %copy.96), calls=%async_computation.7 | async-start | bytes 2097152 | tf_op jit(solution)/shard_map/all_to_all | solution.py:28
  194.9 76.8 %all-reduce.8.cloned.1.call-start = ((), (), s32[]{:S(2)}) async-start(), calls=%async_computation.21 | async-start | bytes 16777216
  195.2 1.1 copy-start.6
  214.7 2.7 copy-start.4
  217.4 99.6 %reduce-scatter.13.cloned.1.call-start = ((), (), s32[]{:S(2)}) async-start(), calls=%async_computation.17 | async-start | bytes 2359296 | tf_op jit(solution)/shard_map/reduce_scatter | solution.py:39
  275.6 87.7 %reduce-scatter.9.cloned.1.call-start = ((), (), s32[]{:S(2)}) async-start(), calls=%async_computation.14 | async-start | bytes 2359296 | tf_op jit(solution)/shard_map/reduce_scatter | solution.py:39
  279.5 1.6 copy-start.1
  283.1 17.4 %copy-start.3 = (bf16[256,16,128]{0,1,2:T(8,128)(2,1)S(1)}, bf16[256,16,128]{0,1,2:T(8,128)(2,1)}, u32[]{:S(2)}) copy-start(bf16[256,16,128]{0,1,2:T(8,128)(2,1)} %copy-done.2) | copy-start | bytes 3145732
  293.1 14.8 %all-to-all-start.3 = ((bf16[256,4,4,32]{0,3,2,1:T(8,128)(2,1)}), bf16[256,4,4,32]{0,3,2,1:T(8,128)(2,1)S(1)}, u32[]{:S(2)}, u32[]{:S(2)}) async-start(bf16[256,4,4,32]{0,3,2,1:T(8,128)(2,1)} %copy.88), calls=%async_computation.3 | async-start | bytes 524288 | tf_op jit(solution)/shard_map/all_to_all | solution.py:28
  299.6 297.9 %all-reduce.6.cloned.1.call-start = ((), (), s32[]{:S(2)}) async-start(), calls=%async_computation.16 | async-start | bytes 524288 | tf_op jit(solution)/shard_map/psum | solution.py:164
  300.4 7.5 %copy-start.10 = (bf16[256,512]{0,1:T(8,128)(2,1)S(1)}, bf16[256,512]{0,1:T(8,128)(2,1)}, u32[]{:S(2)}) copy-start(bf16[256,512]{0,1:T(8,128)(2,1)} %copy.99) | copy-start | bytes 786436
  302.9 297.7 %copy-start.5 = (bf16[256,4,4,128]{0,3,2,1:T(8,128)(2,1)S(1)}, bf16[256,4,4,128]{0,3,2,1:T(8,128)(2,1)}, u32[]{:S(2)}) copy-start(bf16[256,4,4,128]{0,3,2,1:T(8,128)(2,1)} %copy-done.4) | copy-start | bytes 3145732
  309.3 311.0 %reduce-scatter.15.cloned.1.call-start = ((), (), s32[]{:S(2)}) async-start(), calls=%async_computation.18 | async-start | bytes 393216 | tf_op jit(solution)/shard_map/reduce_scatter | solution.py:40
  317.0 326.5 %reduce-scatter.11.cloned.1.call-start = ((), (), s32[]{:S(2)}) async-start(), calls=%async_computation.15 | async-start | bytes 393216 | tf_op jit(solution)/shard_map/reduce_scatter | solution.py:40
Sparse Core Ops, SparseCore 0:
  13.7 42.2 all-gather.12
  58.1 22.8 all-gather.8
  83.0 37.5 all-gather.14
  122.5 22.7 all-gather.10
  217.5 54.1 all-reduce.7
  275.7 41.1 reduce-scatter.12
  319.8 43.4 reduce-scatter.8
  366.7 230.6 all-reduce.5
  601.0 19.2 reduce-scatter.14
  623.5 19.9 reduce-scatter.10
where the time goes:
time: 652 us; the launch traced here: 650 us
  waiting for transfers between devices  509 us (78%)
  blocking collectives  35.8 us (5%)
  local copies, waits for them, and re-layouts  33.3 us (5%)
  starting transfers between devices  31.5 us (5%)
  matrix products  23.7 us (4%)
  between operations  14.3 us (2%)
    psum x1, waiting for transfers between devices, on_device(): rights = lax.psum(rights, DP_AXES)  233 us
    all_gather x2, waiting for transfers between devices, dp_all_gather(): x = lax.all_gather(x, 'z', axis=row_axis, tiled=True)  75 us
    reduce_scatter x2, waiting for transfers between devices, dp_reduce_scatter(): x = lax.psum_scatter(x, 'z', scatter_dimension=row_axis, tiled=True)  53.9 us
    unnamed x11, waiting for transfers between devices  53.1 us
    all_to_all x4, waiting for transfers between devices, exchange(): shaped = lax.all_to_all(shaped, 'yhi', 1, 1, tiled=True)  40.3 us
    reduce_scatter x2, waiting for transfers between devices, dp_reduce_scatter(): x = lax.psum_scatter(x, 'ylo', scatter_dimension=row_axis + 1, tiled=True)  39.8 us
    all_to_all x2, blocking collectives, exchange(): shaped = lax.all_to_all(shaped, 'x', 2, 2, tiled=True)  24.2 us
    all_to_all x4, starting transfers between devices, exchange(): shaped = lax.all_to_all(shaped, 'yhi', 1, 1, tiled=True)  23.7 us
  transfers between devices with their start and end apart: 16, of which 14 were waited for; matrix products, arithmetic and copies ran while one was open for 7% of the time, Pallas kernels for 0%

commit v1 on v0

--- a/solution.py
+++ b/solution.py
@@ -161,7 +161,10 @@
         0,
     ).transpose(1, 0, 2)
     rights = jnp.concatenate([right_up_term, right_down_term], axis=0)
-    rights = lax.psum(rights, DP_AXES)
+    prepare_grid = lambda mat, shard_axis, along_axis: lax.psum(
+        lax.psum(mat, shard_axis), along_axis
+    )
+    rights = prepare_grid(rights, ("ylo", "core"), "z")
     grad_up_right = rights[:group_up]
     grad_down_right = rights[group_up:]
     return (layer_out, grad_tokens, grad_up_left, grad_up_right, grad_down_left, grad_down_right)

time: 652 us -> 549 us (0.84)
  waiting for transfers between devices: 509 us -> 411 us
    psum x1 -> x2, waiting for transfers between devices: 233 us -> 121 us  [the longest x1 78.3 us: on_device(): lax.psum(lax.psum(mat, shard_axis), along_axis)]
    reduce_scatter x2, waiting for transfers between devices: 53.9 us -> 90.7 us  [dp_reduce_scatter(): x = lax.psum_scatter(x, 'z', scatter_dimension=row_axis, tiled=True)]
    unnamed x11 -> x12, waiting for transfers between devices: 53.1 us -> 29 us
  transfers between devices with their start and end apart: 16 -> 17, of which waited for: 14 -> 15; matrix products, arithmetic and copies ran while one was open for 7% -> 8% of each run, Pallas kernels for 0% -> 0%
where the time goes in v1:
time: 549 us; the launch traced here: 548 us
  waiting for transfers between devices  411 us (75%)
  blocking collectives  34.7 us (6%)
  local copies, waits for them, and re-layouts  33.3 us (6%)
  starting transfers between devices  29.1 us (5%)
  matrix products  24 us (4%)
  between operations  14.1 us (3%)
    reduce_scatter x2, waiting for transfers between devices, dp_reduce_scatter(): x = lax.psum_scatter(x, 'z', scatter_dimension=row_axis, tiled=True)  90.7 us
    psum x1, waiting for transfers between devices, on_device(): lax.psum(lax.psum(mat, shard_axis), along_axis)  78.3 us
    all_gather x2, waiting for transfers between devices, dp_all_gather(): x = lax.all_gather(x, 'z', axis=row_axis, tiled=True)  75 us
    reduce_scatter x2, waiting for transfers between devices, dp_reduce_scatter(): x = lax.psum_scatter(x, 'ylo', scatter_dimension=row_axis + 1, tiled=True)  42.9 us
    psum x1, waiting for transfers between devices, on_device(): lax.psum(mat, shard_axis)  42.3 us
    all_to_all x4, waiting for transfers between devices, exchange(): shaped = lax.all_to_all(shaped, 'yhi', 1, 1, tiled=True)  38.2 us
    unnamed x12, waiting for transfers between devices  29 us
    all_to_all x2, blocking collectives, exchange(): shaped = lax.all_to_all(shaped, 'x', 2, 2, tiled=True)  23.1 us
  transfers between devices with their start and end apart: 17, of which 15 were waited for; matrix products, arithmetic and copies ran while one was open for 8% of the time, Pallas kernels for 0%

profile of v1, /device:TPU:1, one launch (start us, length us, event | category | flops | bytes accessed | tf_op | source)
XLA Modules:
  0.0 548.0 jit_solution(1807875059190053653)
XLA Ops:
  7.2 6.3 %all-gather = bf16[2,16,2048]{2,1,0:T(8,128)(2,1)} all-gather(bf16[1,16,2048]{2,1,0:T(8,128)(2,1)} %param.7), channel_id=2, replica_groups=mesh['z'=8,'ylo'=2,'core'=2,'yhi'=4,'x'=4] {'ylo'}, dimensions={0}, use_global_device_ids=true | all-gather | bytes 196608 | tf_op jit(solution)/shard_map/all_gather | solution.py:48
  13.6 42.4 %all-gather.13.cloned.1.call-done = bf16[16,16,2048]{2,1,0:T(8,128)(2,1)} async-done(((bf16[2,16,2048]{2,1,0:T(8,128)(2,1)}), bf16[16,16,2048]{2,1,0:T(8,128)(2,1)}) %all-gather.13.cloned.1.call-update) | async-done | bytes 1048592 | tf_op jit(solution)/shard_map/all_gather | solution.py:49
  56.1 5.3 all-gather.2
  66.9 4.0 all-to-all-start.4
  70.8 10.1 %all-gather.9.cloned.1.call-done = bf16[1,8,2,2,16,2048]{5,4,3,2,1,0:T(8,128)(2,1)} async-done(((bf16[1,8,2,1,16,2048]{5,4,3,2,1,0:T(8,128)(2,1)}), bf16[1,8,2,2,16,2048]{5,4,3,2,1,0:T(8,128)(2,1)}) %all-gather.9.cloned.1.call-update) | async-done | bytes 2097168 | tf_op jit(solution)/shard_map/all_gather | solution.py:50
  84.4 3.5 all-to-all-start
  87.9 32.6 %all-gather.15.cloned.1.call-done = bf16[16,64,512]{2,1,0:T(8,128)(2,1)} async-done(((bf16[2,64,512]{2,1,0:T(8,128)(2,1)}), bf16[16,64,512]{2,1,0:T(8,128)(2,1)}) %all-gather.15.cloned.1.call-update) | async-done | bytes 1048592 | tf_op jit(solution)/shard_map/all_gather | solution.py:49
  121.3 6.5 %all-to-all-start.5 = ((bf16[256,4,4,32]{0,3,2,1:T(8,128)(2,1)}), bf16[256,4,4,32]{0,3,2,1:T(8,128)(2,1)S(1)}, u32[]{:S(2)}, u32[]{:S(2)}) async-start(bf16[256,4,4,32]{0,3,2,1:T(8,128)(2,1)} %copy.91), calls=%async_computation.5 | async-start | bytes 524288 | tf_op jit(solution)/shard_map/all_to_all | solution.py:28
  128.8 6.9 %all-to-all-done.5 = bf16[256,4,4,32]{0,3,2,1:T(8,128)(2,1)S(1)} async-done(((bf16[256,4,4,32]{0,3,2,1:T(8,128)(2,1)}), bf16[256,4,4,32]{0,3,2,1:T(8,128)(2,1)S(1)}, u32[]{:S(2)}, u32[]{:S(2)}) %all-to-all-start.5) | async-done | bytes 262176 | tf_op jit(solution)/shard_map/all_to_all | solution.py:28
  135.7 4.2 all-to-all-start.1
  141.1 4.2 all-gather.11.cloned.1.call-done
  147.6 18.1 %all-to-all-done.1 = bf16[256,4,4,128]{0,3,2,1:T(8,128)(2,1)} async-done(((bf16[256,4,4,128]{0,3,2,1:T(8,128)(2,1)}), bf16[256,4,4,128]{0,3,2,1:T(8,128)(2,1)}, u32[]{:S(2)}, u32[]{:S(2)}) %all-to-all-start.1) | async-done | bytes 1048608 | tf_op jit(solution)/shard_map/all_to_all | solution.py:28
  165.7 4.5 fusion.7
  172.2 15.0 %all_to_all.40 = bf16[256,4,4,128]{0,3,1,2:T(8,128)(2,1)S(1)} all-to-all(bf16[256,4,4,128]{0,3,1,2:T(8,128)(2,1)S(1)} %copy.95), channel_id=1, replica_groups=mesh['z'=8,'ylo'=2,'core'=2,'yhi'=4,'x'=4] {'x'}, dimensions={2} | all-to-all | bytes 2097152 | tf_op jit(solution)/shard_map/all_to_all | solution.py:27
  188.3 6.5 %all-to-all-start.7 = ((bf16[256,4,4,128]{0,3,2,1:T(8,128)(2,1)}), bf16[256,4,4,128]{0,3,2,1:T(8,128)(2,1)S(1)}, u32[]{:S(2)}, u32[]{:S(2)}) async-start(bf16[256,4,4,128]{0,3,2,1:T(8,128)(2,1)} %copy.96), calls=%async_computation.7 | async-start | bytes 2097152 | tf_op jit(solution)/shard_map/all_to_all | solution.py:28
  196.3 2.7 multiply_bitcast_fusion
  199.0 5.4 copy.103
  204.5 10.1 %all-to-all-done.7 = bf16[256,4,4,128]{0,3,2,1:T(8,128)(2,1)S(1)} async-done(((bf16[256,4,4,128]{0,3,2,1:T(8,128)(2,1)}), bf16[256,4,4,128]{0,3,2,1:T(8,128)(2,1)S(1)}, u32[]{:S(2)}, u32[]{:S(2)}) %all-to-all-start.7) | async-done | bytes 1048608 | tf_op jit(solution)/shard_map/all_to_all | solution.py:28
  214.6 2.7 convolution_multiply_fusion
  221.0 8.0 %all_to_all.41 = bf16[256,4,4,32]{0,3,1,2:T(8,128)(2,1)S(1)} all-to-all(bf16[256,4,4,32]{0,3,1,2:T(8,128)(2,1)S(1)} %copy.87), channel_id=1, replica_groups=mesh['z'=8,'ylo'=2,'core'=2,'yhi'=4,'x'=4] {'x'}, dimensions={2} | all-to-all | bytes 524288 | tf_op jit(solution)/shard_map/all_to_all | solution.py:27
  229.8 4.1 all-to-all-start.3
  238.7 3.1 all-to-all-done.3
  243.1 28.8 %all-reduce.11.cloned.1.call-done = (f32[8,2,2,16,1,2048]{5,3,4,2,1,0:T(8,128)}, f32[8,2,2,64,1,512]{5,3,2,1,0,4:T(8,128)}) async-done(((f32[8,2,2,16,1,2048]{5,3,4,2,1,0:T(8,128)}, f32[8,2,2,64,1,512]{5,3,2,1,0,4:T(8,128)}), (f32[8,2,2,16,1,2048]{5,3,4,2,1,0:T(8,128)}, f32[8,2,2,64,1,512]{5,3,2,1,0,4:T(8,128)})) %all-reduce.11.cloned.1.call-update) | async-done | bytes 8388624
  272.0 3.9 constant_dynamic-slice_fusion
  275.9 3.9 constant_dynamic-slice_fusion.1
  279.9 42.3 %all-reduce.7.cloned.1.call-done = f32[160,16,16]{0,2,1:T(8,128)} async-done(((f32[160,16,16]{0,2,1:T(8,128)}), f32[160,16,16]{0,2,1:T(8,128)}) %all-reduce.7.cloned.1.call-update) | async-done | bytes 163856 | tf_op jit(solution)/shard_map/psum | solution.py:165
  322.2 44.2 %reduce-scatter.13.cloned.1.call-done = f32[1,2,1,64,1,512]{5,3,2,1,0,4:T(8,128)} async-done(((f32[8,2,1,64,1,512]{5,3,2,1,0,4:T(8,128)}), f32[1,2,1,64,1,512]{5,3,2,1,0,4:T(8,128)}) %reduce-scatter.13.cloned.1.call-update) | async-done | bytes 262160 | tf_op jit(solution)/shard_map/reduce_scatter | solution.py:39
  366.5 46.5 %reduce-scatter.9.cloned.1.call-done = f32[1,2,1,16,1,2048]{5,3,4,2,1,0:T(8,128)} async-done(((f32[8,2,1,16,1,2048]{5,3,4,2,1,0:T(8,128)}), f32[1,2,1,16,1,2048]{5,3,4,2,1,0:T(8,128)}) %reduce-scatter.9.cloned.1.call-update) | async-done | bytes 262160 | tf_op jit(solution)/shard_map/reduce_scatter | solution.py:39
  414.1 78.3 %all-reduce.9.cloned.1.call-done = f32[160,16,16]{0,2,1:T(8,128)} async-done(((f32[160,16,16]{0,2,1:T(8,128)}), f32[160,16,16]{0,2,1:T(8,128)}) %all-reduce.9.cloned.1.call-update) | async-done | bytes 163856 | tf_op jit(solution)/shard_map/psum | solution.py:164
  495.5 3.0 convolution_convert_fusion.2
  498.6 19.3 %reduce-scatter.15.cloned.1.call-done = f32[1,1,1,64,1,512]{5,3,2,1,0,4:T(8,128)} async-done(((f32[1,2,1,64,1,512]{5,3,2,1,0,4:T(8,128)}), f32[1,1,1,64,1,512]{5,3,2,1,0,4:T(8,128)}) %reduce-scatter.15.cloned.1.call-update) | async-done | bytes 131088 | tf_op jit(solution)/shard_map/reduce_scatter | solution.py:40
  517.9 23.6 %reduce-scatter.11.cloned.1.call-done = f32[1,1,1,16,1,2048]{5,3,4,2,1,0:T(8,128)} async-done(((f32[1,2,1,16,1,2048]{5,3,4,2,1,0:T(8,128)}), f32[1,1,1,16,1,2048]{5,3,4,2,1,0:T(8,128)}) %reduce-scatter.11.cloned.1.call-update) | async-done | bytes 131088 | tf_op jit(solution)/shard_map/reduce_scatter | solution.py:40
  (79 shorter events, 33.9 us)
Async XLA Ops:
  7.2 73.8 %copy-start = (bf16[256,512]{1,0:T(8,128)(2,1)S(1)}, bf16[256,512]{1,0:T(8,128)(2,1)}, u32[]{:S(2)}) copy-start(bf16[256,512]{1,0:T(8,128)(2,1)} %param.6) | copy-start | bytes 786436
  7.2 48.8 %all-gather.13.cloned.1.call-start = ((), (), s32[]{:S(2)}) async-start(), calls=%async_computation.20 | async-start | bytes 1179648 | tf_op jit(solution)/shard_map/all_gather | solution.py:49
  13.6 67.3 %all-gather.9.cloned.1.call-start = ((), (), s32[]{:S(2)}) async-start(), calls=%async_computation.12 | async-start | bytes 3145728 | tf_op jit(solution)/shard_map/all_gather | solution.py:50
  56.0 64.5 %all-gather.15.cloned.1.call-start = ((), (), s32[]{:S(2)}) async-start(), calls=%async_computation.21 | async-start | bytes 1179648 | tf_op jit(solution)/shard_map/all_gather | solution.py:49
  62.3 3.5 copy-start.9
  66.9 17.5 %all-to-all-start.4 = ((bf16[256,4,4,32]{0,3,1,2:T(8,128)(2,1)}), bf16[256,4,4,32]{0,3,1,2:T(8,128)(2,1)S(1)}, u32[]{:S(2)}, u32[]{:S(2)}) async-start(bf16[256,4,4,32]{0,3,1,2:T(8,128)(2,1)} %copy.90), calls=%async_computation.4 | async-start | bytes 524288 | tf_op jit(solution)/shard_map/all_to_all | solution.py:27
  84.4 36.9 %all-to-all-start = ((bf16[256,4,4,128]{0,3,1,2:T(8,128)(2,1)}), bf16[256,4,4,128]{0,3,1,2:T(8,128)(2,1)S(1)}, u32[]{:S(2)}, u32[]{:S(2)}) async-start(bf16[256,4,4,128]{0,3,1,2:T(8,128)(2,1)} %copy.81), calls=%async_computation | async-start | bytes 2097152 | tf_op jit(solution)/shard_map/all_to_all | solution.py:27
  87.9 57.4 %all-gather.11.cloned.1.call-start = ((), (), s32[]{:S(2)}) async-start(), calls=%async_computation.13 | async-start | bytes 3145728 | tf_op jit(solution)/shard_map/all_gather | solution.py:50
  121.3 14.4 %all-to-all-start.5 = ((bf16[256,4,4,32]{0,3,2,1:T(8,128)(2,1)}), bf16[256,4,4,32]{0,3,2,1:T(8,128)(2,1)S(1)}, u32[]{:S(2)}, u32[]{:S(2)}) async-start(bf16[256,4,4,32]{0,3,2,1:T(8,128)(2,1)} %copy.91), calls=%async_computation.5 | async-start | bytes 524288 | tf_op jit(solution)/shard_map/all_to_all | solution.py:28
  127.8 12.2 %copy-start.11 = (bf16[128,16,16]{0,2,1:T(8,128)(2,1)S(1)}, bf16[128,16,16]{0,2,1:T(8,128)(2,1)}, u32[]{:S(2)}) copy-start(bf16[128,16,16]{0,2,1:T(8,128)(2,1)} %param.8) | copy-start | bytes 196612
  135.7 30.0 %all-to-all-start.1 = ((bf16[256,4,4,128]{0,3,2,1:T(8,128)(2,1)}), bf16[256,4,4,128]{0,3,2,1:T(8,128)(2,1)}, u32[]{:S(2)}, u32[]{:S(2)}) async-start(bf16[256,4,4,128]{0,3,2,1:T(8,128)(2,1)} %copy.82), calls=%async_computation.1 | async-start | bytes 2097152 | tf_op jit(solution)/shard_map/all_to_all | solution.py:28
  165.7 5.5 copy-start.7
  170.2 1.0 copy-start.2
  187.2 7.6 %copy-start.8 = (bf16[256,16,128]{0,1,2:T(8,128)(2,1)S(1)}, bf16[256,16,128]{0,1,2:T(8,128)(2,1)}, u32[]{:S(2)}) copy-start(bf16[256,16,128]{0,1,2:T(8,128)(2,1)} %get-tuple-element.21) | copy-start | bytes 3145732
  188.3 26.3 %all-to-all-start.7 = ((bf16[256,4,4,128]{0,3,2,1:T(8,128)(2,1)}), bf16[256,4,4,128]{0,3,2,1:T(8,128)(2,1)S(1)}, u32[]{:S(2)}, u32[]{:S(2)}) async-start(bf16[256,4,4,128]{0,3,2,1:T(8,128)(2,1)} %copy.96), calls=%async_computation.7 | async-start | bytes 2097152 | tf_op jit(solution)/shard_map/all_to_all | solution.py:28
  194.8 77.1 %all-reduce.11.cloned.1.call-start = ((), (), s32[]{:S(2)}) async-start(), calls=%async_computation.22 | async-start | bytes 16777216
  195.2 1.1 copy-start.6
  214.6 2.7 copy-start.4
  217.3 1.6 copy-start.1
  220.8 15.1 %copy-start.3 = (bf16[256,16,128]{0,1,2:T(8,128)(2,1)S(1)}, bf16[256,16,128]{0,1,2:T(8,128)(2,1)}, u32[]{:S(2)}) copy-start(bf16[256,16,128]{0,1,2:T(8,128)(2,1)} %copy-done.2) | copy-start | bytes 3145732
  229.8 12.0 %all-to-all-start.3 = ((bf16[256,4,4,32]{0,3,2,1:T(8,128)(2,1)}), bf16[256,4,4,32]{0,3,2,1:T(8,128)(2,1)S(1)}, u32[]{:S(2)}, u32[]{:S(2)}) async-start(bf16[256,4,4,32]{0,3,2,1:T(8,128)(2,1)} %copy.88), calls=%async_computation.3 | async-start | bytes 524288 | tf_op jit(solution)/shard_map/all_to_all | solution.py:28
  233.8 88.3 %all-reduce.7.cloned.1.call-start = ((), (), s32[]{:S(2)}) async-start(), calls=%async_computation.16 | async-start | bytes 524288 | tf_op jit(solution)/shard_map/psum | solution.py:165
  236.0 5.8 %copy-start.10 = (bf16[256,512]{0,1:T(8,128)(2,1)S(1)}, bf16[256,512]{0,1:T(8,128)(2,1)}, u32[]{:S(2)}) copy-start(bf16[256,512]{0,1:T(8,128)(2,1)} %copy.99) | copy-start | bytes 786436
  243.1 123.3 %reduce-scatter.13.cloned.1.call-start = ((), (), s32[]{:S(2)}) async-start(), calls=%async_computation.18 | async-start | bytes 2359296 | tf_op jit(solution)/shard_map/reduce_scatter | solution.py:39
  275.9 137.2 %reduce-scatter.9.cloned.1.call-start = ((), (), s32[]{:S(2)}) async-start(), calls=%async_computation.14 | async-start | bytes 2359296 | tf_op jit(solution)/shard_map/reduce_scatter | solution.py:39
  279.8 215.7 %copy-start.5 = (bf16[256,4,4,128]{0,3,2,1:T(8,128)(2,1)S(1)}, bf16[256,4,4,128]{0,3,2,1:T(8,128)(2,1)}, u32[]{:S(2)}) copy-start(bf16[256,4,4,128]{0,3,2,1:T(8,128)(2,1)} %copy-done.4) | copy-start | bytes 3145732
  279.8 212.6 %all-reduce.9.cloned.1.call-start = ((), (), s32[]{:S(2)}) async-start(), calls=%async_computation.17 | async-start | bytes 524288 | tf_op jit(solution)/shard_map/psum | solution.py:164
  322.2 195.7 %reduce-scatter.15.cloned.1.call-start = ((), (), s32[]{:S(2)}) async-start(), calls=%async_computation.19 | async-start | bytes 393216 | tf_op jit(solution)/shard_map/reduce_scatter | solution.py:40
  366.5 175.0 %reduce-scatter.11.cloned.1.call-start = ((), (), s32[]{:S(2)}) async-start(), calls=%async_computation.15 | async-start | bytes 393216 | tf_op jit(solution)/shard_map/reduce_scatter | solution.py:40
Sparse Core Ops, SparseCore 0:
  13.7 42.2 all-gather.12
  58.1 22.8 all-gather.8
  83.0 37.5 all-gather.14
  122.5 22.7 all-gather.10
  217.4 54.4 all-reduce.10
  275.3 46.7 all-reduce.6
  325.2 41.1 reduce-scatter.12
  369.5 43.4 reduce-scatter.8
  415.5 76.8 all-reduce.8
  495.6 22.2 reduce-scatter.14
  521.4 19.9 reduce-scatter.10
